TPU v7x, 32 devices: a whole 2x2x4 slice. The times are simulated.
32 devices in a mesh: seq: 4 (over z), ch: 8 (over y, x, core).
Axes of the slice: x: 2, y: 2, z: 4, core: 2. Of those that a mesh axis runs over, the one named last changes fastest.
Arguments:
- inputs: bfloat16 [1024, 8192], P('seq', 'ch'), may hold values from -6 to 6
- w_in: bfloat16 [3, 8192, 8192], P(None, 'seq', 'ch'), may hold values from -0.0625 to 0.0625
- short_filter: float32 [3, 3, 8192], P(None, None, 'ch'), may hold values from -3 to 3
- rates: float32 [16, 8192], P(None, 'ch'), may hold values from 9.765625e-05 to 0.05
- residues: float32 [16, 8192], P(None, 'ch'), may hold values from -3 to 3
- skip: float32 [8192], P('ch'), may hold values from -3 to 3
Outputs:
- gated: bfloat16 [1024, 8192], P('seq', 'ch')
All inputs are finite; a program needn't handle non-finite values.
Results may differ from a plain program's by a relative error of at most 0.0065.
Values may be sent and summed in bfloat16 or wider, within the bound.
No kernel may reach another device: no remote copies, remote signals or barrier semaphores. Data moves between devices by JAX's collectives and lax.ppermute only.
A program may use at most 128 MiB of HBM per device.

v0:
```python
import jax
import jax.numpy as jnp
from jax import lax
from jax.sharding import PartitionSpec as P

TAPS = 3


def passed_along(block, axis, distance):
    devices = range(lax.axis_size(axis))
    route = [(i - distance, i) for i in devices if i - distance in devices]
    return lax.ppermute(block, axis, route)


def carried_in(part, axis, combine, identity):
    place = lax.axis_index(axis)
    gathered = jax.tree.map(lambda a: lax.all_gather(a, axis), part)
    state = jax.tree.map(lambda a, e: jnp.zeros_like(a) + jnp.asarray(e, a.dtype), part, identity)

    def one(hop, state):
        return combine(
            state, jax.tree.map(lambda a: lax.dynamic_index_in_dim(a, hop, 0, False), gathered)
        )

    return lax.fori_loop(0, place, one, state)


def combine(earlier, later):
    return (earlier[0] * later[0], earlier[1] * later[0] + later[1])


def per_device(inputs, w_in, short_filter, rates, residues, skip):
    tok_rows = inputs.shape[0]
    width = w_in.shape[2]
    modes = rates.shape[0]
    features = lax.all_gather(inputs, "ch", axis=1, tiled=True)
    proj = jnp.einsum(
        "td,kdc->ktc",
        features,
        lax.all_gather(w_in, "seq", axis=1, tiled=True),
        preferred_element_type=jnp.float32,
    ).astype(jnp.bfloat16)
    prior = passed_along(proj[:, tok_rows - (TAPS - 1) :, :], "seq", 1)
    padded = jnp.concatenate([prior, proj], axis=1).astype(jnp.float32)
    mixed = jnp.zeros((3, tok_rows, width), jnp.float32)
    for j in range(TAPS):
        mixed = (
            mixed
            + short_filter[:, j, None, :] * padded[:, TAPS - 1 - j : TAPS - 1 - j + tok_rows, :]
        )
    query, key, value = (mixed[0], mixed[1], mixed[2])
    drive = key * value
    position = jnp.arange(tok_rows, dtype=jnp.float32)
    scaled = residues * jnp.sqrt(1.0 - jnp.exp(-2.0 * rates))
    end_powers = jnp.exp(-rates[None, :, :] * (tok_rows - 1.0 - position)[:, None, None])
    end_state = jnp.sum(end_powers * drive[:, None, :], axis=0)
    block_decay = jnp.exp(-rates * tok_rows)
    identity = (jnp.ones_like(block_decay), jnp.zeros_like(end_state))
    entering = carried_in((block_decay, end_state), "seq", combine, identity)[1]
    start_powers = jnp.exp(-rates[None, :, :] * (position + 1.0)[:, None, None])
    cross = jnp.sum(start_powers * (scaled * entering)[None, :, :], axis=1)
    center = (tok_rows - 1.0) / 2.0
    offset = (position - center)[:, None, None]
    rising = jnp.exp(rates[None, :, :] * offset) * drive[:, None, :]
    offsets = jnp.arange(tok_rows, dtype=jnp.int32)
    lower = (offsets[:, None] >= offsets[None, :]).astype(jnp.float32)
    prefix = jnp.dot(
        lower, rising.reshape(tok_rows, modes * width), precision=lax.Precision.HIGHEST
    )
    prefix = prefix.reshape(tok_rows, modes, width)
    falling = jnp.exp(-rates[None, :, :] * offset) * scaled[None, :, :]
    local = jnp.sum(falling * prefix, axis=1)
    return (query * (local + cross + skip[None, :] * drive)).astype(jnp.bfloat16)


def solution(mesh):
    in_specs = (
        P("seq", "ch"),
        P(None, "seq", "ch"),
        P(None, None, "ch"),
        P(None, "ch"),
        P(None, "ch"),
        P("ch"),
    )
    out_specs = P("seq", "ch")
    return jax.shard_map(
        per_device, mesh=mesh, in_specs=in_specs, out_specs=out_specs, check_vma=False
    )
```

profile of v0, /device:TPU:0, one launch (start us, length us, event | category | flops | bytes accessed | tf_op | source)
XLA Modules:
  0.0 979.4 jit_solution(17450163939474768816)
XLA Ops:
  6.5 0.0 all-gather.7.cloned.1.call-start
  6.5 0.7 all-gather.7.cloned.1.call-update
  7.3 0.0 all-gather.5.cloned.1.call-start
  7.3 0.7 all-gather.5.cloned.1.call-update
  8.0 0.9 fusion.17
  9.0 1.5 fusion.16
  10.5 0.0 copy-start
  10.5 38.1 %all-gather.7.cloned.1.call-done = bf16[256,8192]{1,0:T(8,128)(2,1)} async-done(((bf16[256,1024]{1,0:T(8,128)(2,1)}), bf16[256,8192]{1,0:T(8,128)(2,1)}) %all-gather.7.cloned.1.call-update) | async-done | bytes 4194320 | tf_op jit(solution)/shard_map/all_gather | solution.py:36
  48.6 837.6 %all-gather.5.cloned.1.call-done = bf16[3,8192,1024]{2,1,0:T(8,128)(2,1)} async-done(((bf16[3,2048,1024]{2,1,0:T(8,128)(2,1)}), bf16[3,8192,1024]{2,1,0:T(8,128)(2,1)}) %all-gather.5.cloned.1.call-update) | async-done | bytes 50331664 | tf_op jit(solution)/shard_map/all_gather | solution.py:40
  886.2 21.8 %fusion.7 = bf16[3,256,1024]{2,1,0:T(8,128)(2,1)S(1)} fusion(bf16[3,8192,1024]{2,1,0:T(8,128)(2,1)} %all-gather.5.cloned.1.call-done, bf16[256,8192]{1,0:T(8,128)(2,1)} %all-gather.7.cloned.1.call-done), kind=kOutput, calls=%fused_computation.15 | convolution fusion | flops 12885688320 | bytes 56098816 | tf_op jit(solution)/shard_map/td,kdc->ktc/dot_general | solution.py:37
  908.0 1.3 collective-permute-start
  909.3 14.3 %all-gather = f32[64,1024]{1,0:T(8,128)S(1)} all-gather(f32[16,1024]{1,0:T(8,128)S(1)} %get-tuple-element.63), channel_id=2, replica_groups=mesh['seq'=4,'ch'=8] {'seq'}, dimensions={0}, use_global_device_ids=true | all-gather | bytes 327680 | tf_op jit(solution)/shard_map/all_gather | solution.py:17
  923.6 0.0 copy-done
  923.6 0.6 copy.13
  924.3 0.0 collective-permute-done
  924.3 0.5 maximum_convert_fusion
  924.7 0.9 fusion.2
  925.7 1.2 fusion.10
  926.8 2.5 copy.12
  929.4 4.1 multiply_reduce_fusion.1
  933.5 14.6 %all-gather.1 = f32[64,1024]{1,0:T(8,128)} all-gather(f32[16,1024]{1,0:T(8,128)S(1)} %multiply_reduce_fusion.1), channel_id=3, replica_groups=mesh['seq'=4,'ch'=8] {'seq'}, dimensions={0}, use_global_device_ids=true | all-gather | bytes 327680 | tf_op jit(solution)/shard_map/all_gather | solution.py:17
  948.1 0.2 while.12
  948.3 0.0 copy-start.1
  948.3 0.9 fusion.15
  949.2 3.9 bitcast_multiply_fusion.1
  953.1 0.0 copy-start.2
  953.1 0.0 copy-done.1
  953.1 14.0 %multiply_reduce_fusion.2 = f32[256,1024]{1,0:T(8,128)} fusion(f32[16,1024,256]{2,1,0:T(8,128)S(1)} %bitcast.50, f32[16,1024]{1,0:T(8,128)S(1)} %get-tuple-element.61, f32[256]{0:T(256)S(1)} %iota_add_fusion.1, f32[16,1024]{1,0:T(8,128)S(1)} %copy-done.1), kind=kOutput, calls=%fused_computation.5 | convolution fusion | flops 12901482496 | bytes 17957888 | tf_op jit(solution)/shard_map/dot_general | solution.py:67
  967.2 2.8 multiply_reduce_fusion
  970.0 0.0 copy-done.2
  970.0 2.6 fusion.12
  (7 shorter events, 0.1 us)
Async XLA Ops:
  6.5 42.0 %all-gather.7.cloned.1.call-start = ((), (), s32[]{:S(2)}) async-start(), calls=%async_computation.1 | async-start | bytes 4718592 | tf_op jit(solution)/shard_map/all_gather | solution.py:36
  7.3 878.9 %all-gather.5.cloned.1.call-start = ((), (), s32[]{:S(2)}) async-start(), calls=%async_computation | async-start | bytes 62914560 | tf_op jit(solution)/shard_map/all_gather | solution.py:40
  10.5 913.1 %copy-start = (f32[16,1024]{1,0:T(8,128)S(1)}, f32[16,1024]{1,0:T(8,128)}, u32[]{:S(2)}) copy-start(f32[16,1024]{1,0:T(8,128)} %param.11) | copy-start | bytes 196612
  908.0 16.3 %collective-permute-start = (bf16[3,2,1024]{2,1,0:T(2,128)(2,1)S(1)}, bf16[3,2,1024]{2,1,0:T(2,128)(2,1)S(1)}, u32[]{:S(2)}, u32[]{:S(2)}) collective-permute-start(bf16[3,2,1024]{2,1,0:T(2,128)(2,1)S(1)} %slice.40), channel_id=1, source_target_pairs={{0,8},{8,16},{16,24},{1,9},{9,17},{17,25},{2,10},{10,18},{18,26},{... | collective-permute-start | bytes 36872 | tf_op jit(solution)/shard_map/ppermute | solution.py:12
  948.3 4.8 copy-start.1
  953.1 16.9 %copy-start.2 = (f32[1024]{0:T(1024)S(1)}, f32[1024]{0:T(1024)}, u32[]{:S(2)}) copy-start(f32[1024]{0:T(1024)} %param.13) | copy-start | bytes 12292
Sparse Core Ops, SparseCore 0:
  9.2 39.2 all-gather.6
  50.1 835.9 all-gather.4
where the time goes:
time: 980 us; the launch traced here: 979 us
  waiting for transfers between devices  877 us (89%)
  matrix products  35.8 us (4%)
  blocking collectives  28.9 us (3%)
  other arithmetic  18.4 us (2%)
  between operations  13.5 us (1%)
    all_gather x1, waiting for transfers between devices, per_device(): lax.all_gather(w_in, 'seq', axis=1, tiled=True)  838 us
    all_gather x1, waiting for transfers between devices, per_device(): features = lax.all_gather(inputs, 'ch', axis=1, tiled=True)  38.1 us
    all_gather x2, blocking collectives, carried_in(): gathered = jax.tree.map(lambda a: lax.all_gather(a, axis), part)  28.9 us
    dot_general x1, matrix products, per_device(): jnp.einsum('td,kdc->ktc', features, lax.all_gather(w_in, 'seq', axis=1, t...  21.8 us
  transfers between devices with their start and end apart: 3, of which 2 were waited for; matrix products, arithmetic and copies ran while one was open for 0% of the time, Pallas kernels for 0%

commit v1 on v0

--- a/solution.py
+++ b/solution.py
@@ -4,6 +4,18 @@
 from jax.sharding import PartitionSpec as P
 
 TAPS = 3
+
+
+def summed_around(array, axis, dim, product):
+    count, mine, rows = (lax.axis_size(axis), lax.axis_index(axis), array.shape[dim])
+    forward = [(i, (i + 1) % count) for i in range(count)]
+    carried, running = (array, None)
+    for step in range(count):
+        coming = lax.ppermute(carried, axis, forward) if step < count - 1 else None
+        update = product(carried, (mine - step) % count * rows)
+        running = update if running is None else running + update
+        carried = coming
+    return running
 
 
 def passed_along(block, axis, distance):
@@ -34,11 +46,16 @@
     width = w_in.shape[2]
     modes = rates.shape[0]
     features = lax.all_gather(inputs, "ch", axis=1, tiled=True)
-    proj = jnp.einsum(
-        "td,kdc->ktc",
-        features,
-        lax.all_gather(w_in, "seq", axis=1, tiled=True),
-        preferred_element_type=jnp.float32,
+    proj = summed_around(
+        w_in,
+        "seq",
+        1,
+        lambda shard, start: jnp.einsum(
+            "td,kdc->ktc",
+            lax.dynamic_slice_in_dim(features, start, shard.shape[1], axis=1),
+            shard,
+            preferred_element_type=jnp.float32,
+        ),
     ).astype(jnp.bfloat16)
     prior = passed_along(proj[:, tok_rows - (TAPS - 1) :, :], "seq", 1)
     padded = jnp.concatenate([prior, proj], axis=1).astype(jnp.float32)

time: 980 us -> 912 us (0.931)
  waiting for transfers between devices: 877 us -> 796 us
    all_gather x1 -> x0, waiting for transfers between devices: 838 us -> none  [per_device(): lax.all_gather(w_in, 'seq', axis=1, tiled=True)]
    ppermute x0 -> x3, waiting for transfers between devices: none -> 761 us  [summed_around(): coming = lax.ppermute(carried, axis, forward) if step < count - 1 else None]
    dot_general x1 -> x4, matrix products: 21.8 us -> 28.1 us  [per_device(): jnp.einsum('td,kdc->ktc', lax.dynamic_slice_in_dim(features, start, shard...]
  transfers between devices with their start and end apart: 3 -> 5, of which waited for: 2 -> 4; matrix products, arithmetic and copies ran while one was open for 0% -> 3% of each run, Pallas kernels for 0% -> 0%
where the time goes in v1:
time: 912 us; the launch traced here: 911 us
  waiting for transfers between devices  796 us (87%)
  matrix products  42 us (5%)
  blocking collectives  28.7 us (3%)
  other arithmetic  17.1 us (2%)
  between operations  13.7 us (2%)
    ppermute x3, waiting for transfers between devices, summed_around(): coming = lax.ppermute(carried, axis, forward) if step < count - 1 else None  761 us
    all_gather x1, waiting for transfers between devices, per_device(): features = lax.all_gather(inputs, 'ch', axis=1, tiled=True)  35.4 us
    all_gather x2, blocking collectives, carried_in(): gathered = jax.tree.map(lambda a: lax.all_gather(a, axis), part)  28.7 us
    dot_general x4, matrix products, per_device(): jnp.einsum('td,kdc->ktc', lax.dynamic_slice_in_dim(features, start, shard...  28.1 us
  transfers between devices with their start and end apart: 5, of which 4 were waited for; matrix products, arithmetic and copies ran while one was open for 3% of the time, Pallas kernels for 0%

profile of v1, /device:TPU:0, one launch (start us, length us, event | category | flops | bytes accessed | tf_op | source)
XLA Modules:
  0.0 911.2 jit_solution(17279165955757633357)
XLA Ops:
  6.5 3.1 collective-permute-start
  9.6 272.6 %collective-permute-done = bf16[3,2048,1024]{2,1,0:T(8,128)(2,1)S(1)} collective-permute-done((bf16[3,2048,1024]{2,1,0:T(8,128)(2,1)}, bf16[3,2048,1024]{2,1,0:T(8,128)(2,1)S(1)}, u32[]{:S(2)}, u32[]{:S(2)}) %collective-permute-start) | collective-permute-done | bytes 12582944 | tf_op jit(solution)/shard_map/ppermute | solution.py:14
  282.2 4.6 copy-done
  286.8 0.0 collective-permute-start.1
  286.8 273.4 %collective-permute-done.1 = bf16[3,2048,1024]{2,1,0:T(8,128)(2,1)} collective-permute-done((bf16[3,2048,1024]{2,1,0:T(8,128)(2,1)S(1)}, bf16[3,2048,1024]{2,1,0:T(8,128)(2,1)}, u32[]{:S(2)}, u32[]{:S(2)}) %collective-permute-start.1) | collective-permute-done | bytes 12582944 | tf_op jit(solution)/shard_map/ppermute | solution.py:14
  560.2 0.0 collective-permute-start.2
  560.2 0.0 all-gather.4.cloned.1.call-update
  560.3 0.9 fusion.25
  561.3 1.5 fusion.24
  562.8 35.4 %all-gather.4.cloned.1.call-done = bf16[256,8192]{1,0:T(8,128)(2,1)} async-done(((bf16[256,1024]{1,0:T(8,128)(2,1)}), bf16[256,8192]{1,0:T(8,128)(2,1)}) %all-gather.4.cloned.1.call-update) | async-done | bytes 4194320 | tf_op jit(solution)/shard_map/all_gather | solution.py:48
  598.2 6.9 fusion.11
  605.1 6.4 fusion.9
  611.5 6.4 fusion.7
  618.0 0.0 copy-start.3
  618.0 215.0 %collective-permute-done.2 = bf16[3,2048,1024]{2,1,0:T(8,128)(2,1)} collective-permute-done((bf16[3,2048,1024]{2,1,0:T(8,128)(2,1)}, bf16[3,2048,1024]{2,1,0:T(8,128)(2,1)}, u32[]{:S(2)}, u32[]{:S(2)}) %collective-permute-start.2) | collective-permute-done | bytes 12582944 | tf_op jit(solution)/shard_map/ppermute | solution.py:14
  832.9 8.3 fusion.2
  841.3 1.3 collective-permute-start.3
  842.6 13.8 %all-gather = f32[64,1024]{1,0:T(8,128)S(1)} all-gather(f32[16,1024]{1,0:T(8,128)S(1)} %get-tuple-element.63), channel_id=2, replica_groups=mesh['seq'=4,'ch'=8] {'seq'}, dimensions={0}, use_global_device_ids=true | all-gather | bytes 327680 | tf_op jit(solution)/shard_map/all_gather | solution.py:29
  856.4 0.6 copy.13
  857.0 0.0 collective-permute-done.3
  857.0 0.5 maximum_convert_fusion
  857.5 0.9 fusion
  858.4 1.2 fusion.3
  859.6 2.5 copy.12
  862.1 4.1 multiply_reduce_fusion.1
  866.3 14.9 %all-gather.1 = f32[64,1024]{1,0:T(8,128)} all-gather(f32[16,1024]{1,0:T(8,128)S(1)} %multiply_reduce_fusion.1), channel_id=3, replica_groups=mesh['seq'=4,'ch'=8] {'seq'}, dimensions={0}, use_global_device_ids=true | all-gather | bytes 327680 | tf_op jit(solution)/shard_map/all_gather | solution.py:29
  881.2 0.2 while.12
  881.4 0.9 fusion.23
  882.2 3.9 bitcast_multiply_fusion.1
  886.2 14.0 %multiply_reduce_fusion.2 = f32[256,1024]{1,0:T(8,128)} fusion(f32[16,1024,256]{2,1,0:T(8,128)S(1)} %bitcast.58, f32[16,1024]{1,0:T(8,128)S(1)} %get-tuple-element.61, f32[256]{0:T(256)S(1)} %iota_add_fusion.1, f32[16,1024]{1,0:T(8,128)S(1)} %copy-done.5), kind=kOutput, calls=%fused_computation.5 | convolution fusion | flops 12901482496 | bytes 17957888 | tf_op jit(solution)/shard_map/dot_general | solution.py:84
  900.2 2.8 multiply_reduce_fusion
  903.0 1.4 fusion.5
  (20 shorter events, 0.1 us)
Async XLA Ops:
  6.5 591.6 %all-gather.4.cloned.1.call-start = ((), (), s32[]{:S(2)}) async-start(), calls=%async_computation | async-start | bytes 4718592 | tf_op jit(solution)/shard_map/all_gather | solution.py:48
  6.5 275.6 %collective-permute-start = (bf16[3,2048,1024]{2,1,0:T(8,128)(2,1)}, bf16[3,2048,1024]{2,1,0:T(8,128)(2,1)S(1)}, u32[]{:S(2)}, u32[]{:S(2)}) collective-permute-start(bf16[3,2048,1024]{2,1,0:T(8,128)(2,1)} %param.9), channel_id=1, source_target_pairs={{0,8},{8,16},{16,24},{24,0},{1,9},{9,17},{17,25},{25,1},{2,10},{10... | collective-permute-start | bytes 37748744 | tf_op jit(solution)/shard_map/ppermute | solution.py:14
  282.2 4.6 copy-start
  286.8 273.4 %collective-permute-start.1 = (bf16[3,2048,1024]{2,1,0:T(8,128)(2,1)S(1)}, bf16[3,2048,1024]{2,1,0:T(8,128)(2,1)}, u32[]{:S(2)}, u32[]{:S(2)}) collective-permute-start(bf16[3,2048,1024]{2,1,0:T(8,128)(2,1)S(1)} %collective-permute-done), channel_id=1, source_target_pairs={{0,8},{8,16},{16,24},{24,0},{1,9},{9,17},{17,25},{25,1},{2,10},{10... | collective-permute-start | bytes 37748744 | tf_op jit(solution)/shard_map/ppermute | solution.py:14
  560.2 272.8 %collective-permute-start.2 = (bf16[3,2048,1024]{2,1,0:T(8,128)(2,1)}, bf16[3,2048,1024]{2,1,0:T(8,128)(2,1)}, u32[]{:S(2)}, u32[]{:S(2)}) collective-permute-start(bf16[3,2048,1024]{2,1,0:T(8,128)(2,1)} %collective-permute-done.1), channel_id=1, source_target_pairs={{0,8},{8,16},{16,24},{24,0},{1,9},{9,17},{17,25},{25,1},{2,10},{10... | collective-permute-start | bytes 37748744 | tf_op jit(solution)/shard_map/ppermute | solution.py:14
  598.2 6.9 copy-start.1
  618.0 238.4 %copy-start.3 = (f32[16,1024]{1,0:T(8,128)S(1)}, f32[16,1024]{1,0:T(8,128)}, u32[]{:S(2)}) copy-start(f32[16,1024]{1,0:T(8,128)} %param.11) | copy-start | bytes 196612
  841.3 15.8 %collective-permute-start.3 = (bf16[3,2,1024]{2,1,0:T(2,128)(2,1)S(1)}, bf16[3,2,1024]{2,1,0:T(2,128)(2,1)S(1)}, u32[]{:S(2)}, u32[]{:S(2)}) collective-permute-start(bf16[3,2,1024]{2,1,0:T(2,128)(2,1)S(1)} %slice.40), channel_id=1, source_target_pairs={{0,8},{8,16},{16,24},{1,9},{9,17},{17,25},{2,10},{10,18},{18,26},{... | collective-permute-start | bytes 36872 | tf_op jit(solution)/shard_map/ppermute | solution.py:24
  858.4 3.7 copy-start.4
  882.2 3.9 copy-start.5
  900.2 2.8 copy-start.2
  900.2 2.8 copy-start.6
Sparse Core Ops, SparseCore 0:
  560.3 37.8 all-gather.3
